TPU v7x, 128 devices: a whole 4x4x4 slice. The times are simulated.
128 devices in a mesh: seq: 32 (over z, y, core), tp: 4 (over x).
Axes of the slice: x: 4, y: 4, z: 4, core: 2. Of those that a mesh axis runs over, the one named last changes fastest.
Arguments:
- tokens: bfloat16 [16384, 1408], P('seq'), may hold values from -70 to 70
- group_image: int32 [4096], P('seq'), may hold values from 0 to 31, never falling along the last dimension, each value on 1 to 512 neighbouring positions
- image_slot: int32 [32], replicated, may hold values from 0 to 31, each once
- attention_gain: float32 [1408], replicated, may hold values from 0.1 to 1.9
- query_weight: bfloat16 [1408, 1408], P(None, 'tp'), may hold values from -1.11930376 to 1.11930376
- key_weight: bfloat16 [1408, 1408], P(None, 'tp'), may hold values from -1.11930376 to 1.11930376
- value_weight: bfloat16 [1408, 1408], P(None, 'tp'), may hold values from -1.25 to 1.25
- output_weight: bfloat16 [1408, 1408], P('tp'), may hold values from -0.15625 to 0.15625
- feedforward_gain: float32 [1408], replicated, may hold values from 0.1 to 1.9
- up_weight: bfloat16 [1408, 6144], P(None, 'tp'), may hold values from -0.15625 to 0.15625
- down_weight: bfloat16 [6144, 1408], P('tp'), may hold values from -0.078125 to 0.078125
- merge_gain: float32 [1408], replicated, may hold values from 0.1 to 1.9
- merge_weight: bfloat16 [5632, 3584], P(None, 'tp'), may hold values from -0.078125 to 0.078125
Outputs:
- merged_rows: bfloat16 [32, 512, 3584], P('seq', None, 'tp')
Inputs may be any that keep to these rules, and one draw needn't show every extreme that they name: `group_image`: images are numbered in the order of their groups, each covers consecutive groups, 1 to 512 of them, and one covers exactly 512.
All inputs are finite; a program needn't handle non-finite values.
Results may differ from a plain program's by a relative error of at most 0.012.
Values may be sent and summed in bfloat16 or wider, within the bound.
No kernel may reach another device: no remote copies, remote signals or barrier semaphores. Data moves between devices by JAX's collectives and lax.ppermute only.
A program may use at most 192 MiB of HBM per device.

v0:
```python
import jax
import jax.numpy as jnp
from jax import lax
from jax.sharding import PartitionSpec as P

D = 1408
HD = 88
REACH = 4
epsilon = 1e-06
masked_score = -1e30


def shifted(value, axis, steps):
    count = lax.axis_size(axis)
    initial, last = (max(0, -steps), min(count, count - steps))
    return lax.ppermute(value, axis, [(source, source + steps) for source in range(initial, last)])


def finish_norm(hidden, row_mean, square, norm_gain):
    return (
        (hidden - row_mean) * lax.rsqrt(square - row_mean * row_mean + epsilon) * norm_gain
    ).astype(jnp.bfloat16)


def full_norm(hidden, norm_gain):
    row_mean = jnp.mean(hidden, axis=1, keepdims=True)
    square = jnp.mean(hidden * hidden, axis=1, keepdims=True)
    return finish_norm(hidden, row_mean, square, norm_gain)


def sum_rows(partial_value):
    return lax.psum(partial_value, "tp")


def attend_window(query_heads, key_heads, value_heads, query_image, key_image):
    scores = jnp.einsum(
        "qhd,khd->hqk", query_heads, key_heads, preferred_element_type=jnp.float32
    ) * HD ** (-0.5)
    same_image = query_image[:, None] == key_image[None, :]
    scores = jnp.where(same_image[None], scores, masked_score)
    row_best = jnp.max(scores, axis=2, keepdims=True)
    weights = jnp.exp(scores - row_best)
    row_total = jnp.sum(weights, axis=2)
    weighted = jnp.einsum(
        "hqk,khd->qhd",
        weights.astype(jnp.bfloat16),
        value_heads,
        preferred_element_type=jnp.float32,
    )
    return weighted / jnp.transpose(row_total)[:, :, None]


def shards(
    tokens,
    group_image,
    image_slot,
    attention_gain,
    query_weight,
    key_weight,
    value_weight,
    output_weight,
    feedforward_gain,
    up_weight,
    down_weight,
    merge_gain,
    merge_weight,
):
    device = lax.axis_index("seq")
    seq_count = lax.axis_size("seq")
    token_rows = tokens.shape[0]
    group_rows = group_image.shape[0]
    group_table = lax.all_gather(group_image, "seq", axis=0, tiled=True)
    token_image = jnp.repeat(group_table, 4)
    query_image = lax.dynamic_slice_in_dim(token_image, device * token_rows, token_rows, 0)
    residual = tokens.astype(jnp.float32)
    normed = full_norm(residual, attention_gain)
    head_count = query_weight.shape[1] // HD
    queries = jnp.dot(normed, query_weight, preferred_element_type=jnp.float32).astype(jnp.bfloat16)
    key_rows = jnp.dot(normed, key_weight, preferred_element_type=jnp.float32).astype(jnp.bfloat16)
    value_rows = jnp.dot(normed, value_weight, preferred_element_type=jnp.float32).astype(
        jnp.bfloat16
    )
    query_heads = queries.reshape(token_rows, head_count, HD)
    key_value = jnp.stack([key_rows, value_rows])
    arrived = []
    for offset in range(REACH, -REACH - 1, -1):
        if offset == 0:
            arrived.append(key_value)
        else:
            arrived.append(shifted(key_value, "seq", offset))
    window = jnp.concatenate(arrived, axis=1)
    reach_rows = REACH * token_rows
    image_pad = jnp.full((reach_rows,), -1, jnp.int32)
    image_padded = jnp.concatenate([image_pad, token_image, image_pad], axis=0)
    key_image = lax.dynamic_slice_in_dim(
        image_padded, device * token_rows, (2 * REACH + 1) * token_rows, 0
    )
    context = attend_window(
        query_heads,
        window[0].reshape(-1, head_count, HD),
        window[1].reshape(-1, head_count, HD),
        query_image,
        key_image,
    )
    context = context.astype(jnp.bfloat16).reshape(token_rows, head_count * HD)
    attention_part = jnp.dot(context, output_weight, preferred_element_type=jnp.float32)
    after_attention = residual + sum_rows(attention_part)
    normed_two = full_norm(after_attention, feedforward_gain)
    hidden_units = jax.nn.gelu(
        jnp.dot(normed_two, up_weight, preferred_element_type=jnp.float32), approximate=False
    ).astype(jnp.bfloat16)
    after_feedforward = after_attention + sum_rows(
        jnp.dot(hidden_units, down_weight, preferred_element_type=jnp.float32)
    )
    normed_three = full_norm(after_feedforward, merge_gain)
    grouped = normed_three.reshape(group_rows, 4 * D)
    projected = jnp.dot(grouped, merge_weight, preferred_element_type=jnp.float32).astype(
        jnp.bfloat16
    )
    image_count = image_slot.shape[0]
    image_ids = jnp.arange(image_count, dtype=jnp.int32)
    own_image = jnp.sum(jnp.where(image_slot == device, image_ids, 0))
    first_group = jnp.sum((group_table < own_image).astype(jnp.int32))
    group_count = jnp.sum((group_table == own_image).astype(jnp.int32))
    most_rows = REACH * group_rows
    row_numbers = jnp.arange(most_rows, dtype=jnp.int32)
    kept_rows = row_numbers < group_count
    out_cols = projected.shape[1]
    my_images = lax.dynamic_slice_in_dim(group_table, device * group_rows, group_rows, 0)
    target = jnp.sum(
        jnp.where(my_images[:, None] == image_ids[None, :], image_slot[None, :], 0), axis=1
    )
    owners = jnp.arange(seq_count, dtype=jnp.int32)
    outgoing = jnp.where(
        (target[None, :] == owners[:, None])[:, :, None],
        projected[None],
        jnp.zeros((), jnp.bfloat16),
    )
    received = lax.all_to_all(outgoing, "seq", split_axis=0, concat_axis=0, tiled=True).reshape(
        seq_count * group_rows, out_cols
    )
    padded = jnp.concatenate([received, jnp.zeros((most_rows, out_cols), jnp.bfloat16)], axis=0)
    own_block = lax.dynamic_slice_in_dim(padded, first_group, most_rows, 0)
    return jnp.where(kept_rows[:, None], own_block, jnp.zeros((), jnp.bfloat16))[None]


def solution(mesh):
    return jax.shard_map(
        shards,
        mesh=mesh,
        in_specs=(
            P("seq", None),
            P("seq"),
            P(),
            P(),
            P(None, "tp"),
            P(None, "tp"),
            P(None, "tp"),
            P("tp", None),
            P(),
            P(None, "tp"),
            P("tp", None),
            P(),
            P(None, "tp"),
        ),
        out_specs=P("seq", None, "tp"),
        check_vma=False,
    )
```

profile of v0, /device:TPU:0, one launch (start us, length us, event | category | flops | bytes accessed | tf_op | source)
XLA Modules:
  0.0 497.9 jit_solution(5010891190266689677)
XLA Ops:
  6.5 2.0 convert_reduce_fusion
  8.6 1.9 fusion.18
  15.2 3.9 collective-permute-start.3
  19.2 3.6 collective-permute-start.2
  22.7 3.9 collective-permute-start.1
  26.6 5.6 %collective-permute-start = (bf16[2,512,352]{1,2,0:T(8,128)(2,1)}, bf16[2,512,352]{1,2,0:T(8,128)(2,1)}, u32[]{:S(2)}, u32[]{:S(2)}) collective-permute-start(bf16[2,512,352]{1,2,0:T(8,128)(2,1)} %pad_maximum_fusion), channel_id=1, source_target_pairs={{0,16},{4,20},{8,24},{12,28},{16,32},{20,36},{24,40},{28,44},{32,4... | collective-permute-start | bytes 2162696 | tf_op jit(solution)/shard_map/ppermute | solution.py:16
  32.2 62.3 %all-gather = s32[32,1,128]{2,1,0:T(1,128)S(1)} all-gather(s32[1,1,128]{2,1,0:T(1,128)S(1)} %bitcast.42), channel_id=1, replica_groups=mesh['seq'=32,'tp'=4] {'seq'}, dimensions={0}, use_global_device_ids=true | all-gather | bytes 16896 | tf_op jit(solution)/shard_map/all_gather | solution.py:72
  95.1 1.6 reshape.126
  98.3 3.2 convolution_convert_fusion
  101.5 1.4 collective-permute-start.5
  106.5 1.5 collective-permute-start.7
  111.6 11.1 %collective-permute-done.5 = bf16[2,512,352]{1,2,0:T(8,128)(2,1)S(1)} collective-permute-done((bf16[2,512,352]{1,2,0:T(8,128)(2,1)}, bf16[2,512,352]{1,2,0:T(8,128)(2,1)S(1)}, u32[]{:S(2)}, u32[]{:S(2)}) %collective-permute-start.5) | collective-permute-done | bytes 720928 | tf_op jit(solution)/shard_map/ppermute | solution.py:16
  122.7 7.1 %collective-permute-done.6 = bf16[2,512,352]{1,2,0:T(8,128)(2,1)S(1)} collective-permute-done((bf16[2,512,352]{1,2,0:T(8,128)(2,1)}, bf16[2,512,352]{1,2,0:T(8,128)(2,1)S(1)}, u32[]{:S(2)}, u32[]{:S(2)}) %collective-permute-start.6) | collective-permute-done | bytes 720928 | tf_op jit(solution)/shard_map/ppermute | solution.py:16
  129.8 4.5 collective-permute-done.7
  134.4 3.1 fusion.109
  137.6 18.3 %fusion = (f32[4,512]{1,0:T(4,128)S(1)}, f32[4,512,4608]{2,1,0:T(8,128)}) fusion(pred[512,4608]{1,0:T(8,128)(4,1)S(1)} %broadcast_compare_fusion, bf16[512,4,88]{0,2,1:T(8,128)(2,1)S(1)} %bitcast.43, bf16[4608,4,88]{0,2,1:T(8,128)(2,1)} %bitcast.36), kind=kOutput, calls=%fused_computation.2 | convolution fusion | flops 1689253888 | bytes 43720704 | tf_op jit(solution)/shard_map/qhd,khd->hqk/dot_general | solution.py:36
  155.8 17.5 %fusion.1 = f32[4,512]{1,0:T(4,128)S(1)} fusion(f32[4,512,4608]{2,1,0:T(8,128)} %get-tuple-element.23, f32[4,512]{1,0:T(4,128)S(1)} %get-tuple-element.22, pred[512,4608]{1,0:T(8,128)(4,1)S(1)} %broadcast_compare_fusion), kind=kLoop, calls=%fused_computation.3 | loop fusion | flops 37746688 | bytes 40124416 | tf_op jit(solution)/shard_map/reduce_sum | solution.py:43
  173.3 15.3 %fusion.67 = bf16[512,4,88]{0,2,1:T(8,128)(2,1)S(1)} fusion(bf16[4608,4,88]{0,2,1:T(8,128)(2,1)S(1)} %bitcast.35, f32[4,512,4608]{2,1,0:T(8,128)} %get-tuple-element.23, f32[4,512]{1,0:T(4,128)S(1)} %get-tuple-element.22, pred[512,4608]{1,0:T(8,128)(4,1)S(1)} %broadcast_compare_fusion, f32[512,4]{0,1:T(4,128)S(1)} %bitcast.41), kind=kOutput, calls=%fused_computation.84 | convolution fusion | flops 1699053568 | bytes 43728896 | tf_op jit(solution)/shard_map/hqk,khd->qhd/dot_general | solution.py:44
  188.6 2.6 fusion.110
  191.5 90.3 %all-reduce.4.cloned.1.call-done = f32[512,1408]{1,0:T(8,128)} async-done(((f32[512,1408]{1,0:T(8,128)}), f32[512,1408]{1,0:T(8,128)}) %all-reduce.4.cloned.1.call-update) | async-done | bytes 2883600 | tf_op jit(solution)/shard_map/psum | solution.py:32
  281.8 2.5 fusion.71
  284.3 16.3 %fusion.20 = f32[512,1408]{1,0:T(8,128)} fusion(bf16[1536,1408]{1,0:T(8,128)(2,1)} %param.23, bf16[1408,1536]{1,0:T(8,128)(2,1)} %param.22, f32[1408]{0:T(1024)S(1)} %copy-done.11, f32[512]{0:T(512)S(1)} %get-tuple-element.19, f32[512]{0:T(512)S(1)} %get-tuple-element.18, f32[512,1408]{1,0:T(8,128)} %all-reduce.4.cloned.1.call-done, ...), kind=kOutput, calls=%fused_computation.41 | convolution fusion | flops 4484628480 | bytes 15869440 | tf_op jit(solution)/shard_map/dot_general | solution.py:113
  300.8 71.2 %all-reduce.6.cloned.1.call-done = f32[512,1408]{1,0:T(8,128)} async-done(((f32[512,1408]{1,0:T(8,128)}), f32[512,1408]{1,0:T(8,128)}) %all-reduce.6.cloned.1.call-update) | async-done | bytes 2883600 | tf_op jit(solution)/shard_map/psum | solution.py:32
  372.0 3.4 fusion.107
  375.5 1.6 multiply_convert_fusion
  377.0 2.7 reshape.129
  379.7 5.5 %convolution_convert_fusion.3 = bf16[128,896]{1,0:T(8,128)(2,1)S(1)} fusion(bf16[128,5632]{1,0:T(8,128)(2,1)S(1)} %reshape.129, bf16[5632,896]{1,0:T(8,128)(2,1)} %param.25), kind=kOutput, calls=%fused_computation.82 | convolution fusion | flops 1291960320 | bytes 11763712 | tf_op jit(solution)/shard_map/dot_general | solution.py:117
  385.2 3.8 broadcast_select_fusion
  389.1 7.4 %all-to-all-start = ((bf16[32,128,896]{2,1,0:T(8,128)(2,1)}), bf16[32,128,896]{2,1,0:T(8,128)(2,1)}, u32[]{:S(2)}, u32[]{:S(2)}) async-start(bf16[32,128,896]{2,1,0:T(8,128)(2,1)} %broadcast_select_fusion), calls=%async_computation | async-start | bytes 14680064 | tf_op jit(solution)/shard_map/all_to_all | solution.py:139
  397.1 1.4 convert_reduce_fusion.2
  401.2 87.6 %all-to-all-done = bf16[32,128,896]{2,1,0:T(8,128)(2,1)} async-done(((bf16[32,128,896]{2,1,0:T(8,128)(2,1)}), bf16[32,128,896]{2,1,0:T(8,128)(2,1)}, u32[]{:S(2)}, u32[]{:S(2)}) %all-to-all-start) | async-done | bytes 7340064 | tf_op jit(solution)/shard_map/all_to_all | solution.py:139
  488.7 2.3 select_bitcast_fusion
  (64 shorter events, 15.9 us)
Async XLA Ops:
  6.5 182.1 %copy-start = (bf16[352,1408]{1,0:T(8,128)(2,1)S(1)}, bf16[352,1408]{1,0:T(8,128)(2,1)}, u32[]{:S(2)}) copy-start(bf16[352,1408]{1,0:T(8,128)(2,1)} %param.20) | copy-start | bytes 2973700
  6.5 3.9 copy-start.9
  6.5 275.3 %all-reduce.4.cloned.1.call-start = ((), (), s32[]{:S(2)}) async-start(), calls=%async_computation.1 | async-start | bytes 5767168 | tf_op jit(solution)/shard_map/psum | solution.py:32
  10.5 2.5 copy-start.4
  10.5 1.7 copy-start.10
  12.2 20.1 %copy-start.8 = (s32[128]{0:T(128)S(1)}, s32[128]{0:T(128)}, u32[]{:S(2)}) copy-start(s32[128]{0:T(128)} %param.14) | copy-start | bytes 1540
  13.0 1.0 copy-start.5
  14.0 96.5 %collective-permute-start.4 = (bf16[2,512,352]{1,2,0:T(8,128)(2,1)}, bf16[2,512,352]{1,2,0:T(8,128)(2,1)}, u32[]{:S(2)}, u32[]{:S(2)}) collective-permute-start(bf16[2,512,352]{1,2,0:T(8,128)(2,1)} %pad_maximum_fusion), channel_id=1, source_target_pairs={{4,0},{8,4},{12,8},{16,12},{20,16},{24,20},{28,24},{32,28},{36,32}... | collective-permute-start | bytes 2162696 | tf_op jit(solution)/shard_map/ppermute | solution.py:16
  15.2 93.9 %collective-permute-start.3 = (bf16[2,512,352]{1,2,0:T(8,128)(2,1)}, bf16[2,512,352]{1,2,0:T(8,128)(2,1)}, u32[]{:S(2)}, u32[]{:S(2)}) collective-permute-start(bf16[2,512,352]{1,2,0:T(8,128)(2,1)} %pad_maximum_fusion), channel_id=1, source_target_pairs={{0,4},{4,8},{8,12},{12,16},{16,20},{20,24},{24,28},{28,32},{32,36}... | collective-permute-start | bytes 2162696 | tf_op jit(solution)/shard_map/ppermute | solution.py:16
  19.2 87.4 %collective-permute-start.2 = (bf16[2,512,352]{1,2,0:T(8,128)(2,1)}, bf16[2,512,352]{1,2,0:T(8,128)(2,1)}, u32[]{:S(2)}, u32[]{:S(2)}) collective-permute-start(bf16[2,512,352]{1,2,0:T(8,128)(2,1)} %pad_maximum_fusion), channel_id=1, source_target_pairs={{0,8},{4,12},{8,16},{12,20},{16,24},{20,28},{24,32},{28,36},{32,40... | collective-permute-start | bytes 2162696 | tf_op jit(solution)/shard_map/ppermute | solution.py:16
  22.7 81.3 %collective-permute-start.1 = (bf16[2,512,352]{1,2,0:T(8,128)(2,1)}, bf16[2,512,352]{1,2,0:T(8,128)(2,1)}, u32[]{:S(2)}, u32[]{:S(2)}) collective-permute-start(bf16[2,512,352]{1,2,0:T(8,128)(2,1)} %pad_maximum_fusion), channel_id=1, source_target_pairs={{0,12},{4,16},{8,20},{12,24},{16,28},{20,32},{24,36},{28,40},{32,4... | collective-permute-start | bytes 2162696 | tf_op jit(solution)/shard_map/ppermute | solution.py:16
  26.6 74.9 %collective-permute-start = (bf16[2,512,352]{1,2,0:T(8,128)(2,1)}, bf16[2,512,352]{1,2,0:T(8,128)(2,1)}, u32[]{:S(2)}, u32[]{:S(2)}) collective-permute-start(bf16[2,512,352]{1,2,0:T(8,128)(2,1)} %pad_maximum_fusion), channel_id=1, source_target_pairs={{0,16},{4,20},{8,24},{12,28},{16,32},{20,36},{24,40},{28,44},{32,4... | collective-permute-start | bytes 2162696 | tf_op jit(solution)/shard_map/ppermute | solution.py:16
  101.5 8.9 %copy-start.6 = (bf16[1,512,352]{1,2,0:T(8,128)(2,1)S(1)}, bf16[1,512,352]{1,2,0:T(8,128)(2,1)}, u32[]{:S(2)}) copy-start(bf16[1,512,352]{1,2,0:T(8,128)(2,1)} %copy-done.5) | copy-start | bytes 1081348
  101.5 21.2 %collective-permute-start.5 = (bf16[2,512,352]{1,2,0:T(8,128)(2,1)}, bf16[2,512,352]{1,2,0:T(8,128)(2,1)S(1)}, u32[]{:S(2)}, u32[]{:S(2)}) collective-permute-start(bf16[2,512,352]{1,2,0:T(8,128)(2,1)} %pad_maximum_fusion), channel_id=1, source_target_pairs={{8,0},{12,4},{16,8},{20,12},{24,16},{28,20},{32,24},{36,28},{40,32... | collective-permute-start | bytes 2162696 | tf_op jit(solution)/shard_map/ppermute | solution.py:16
  104.1 25.7 %collective-permute-start.6 = (bf16[2,512,352]{1,2,0:T(8,128)(2,1)}, bf16[2,512,352]{1,2,0:T(8,128)(2,1)S(1)}, u32[]{:S(2)}, u32[]{:S(2)}) collective-permute-start(bf16[2,512,352]{1,2,0:T(8,128)(2,1)} %pad_maximum_fusion), channel_id=1, source_target_pairs={{12,0},{16,4},{20,8},{24,12},{28,16},{32,20},{36,24},{40,28},{44,3... | collective-permute-start | bytes 2162696 | tf_op jit(solution)/shard_map/ppermute | solution.py:16
  106.5 27.8 %collective-permute-start.7 = (bf16[2,512,352]{1,2,0:T(8,128)(2,1)}, bf16[2,512,352]{1,2,0:T(8,128)(2,1)S(1)}, u32[]{:S(2)}, u32[]{:S(2)}) collective-permute-start(bf16[2,512,352]{1,2,0:T(8,128)(2,1)} %pad_maximum_fusion), channel_id=1, source_target_pairs={{16,0},{20,4},{24,8},{28,12},{32,16},{36,20},{40,24},{44,28},{48,3... | collective-permute-start | bytes 2162696 | tf_op jit(solution)/shard_map/ppermute | solution.py:16
  134.4 3.2 copy-start.13
  155.8 17.5 %copy-start.3 = (bf16[1,4608,352]{1,2,0:T(8,128)(2,1)S(1)}, bf16[1,4608,352]{1,2,0:T(8,128)(2,1)}, u32[]{:S(2)}) copy-start(bf16[1,4608,352]{1,2,0:T(8,128)(2,1)} %get-tuple-element.15) | copy-start | bytes 9732100
  188.6 93.2 %copy-start.2 = (bf16[512,1408]{1,0:T(8,128)(2,1)S(1)}, bf16[512,1408]{1,0:T(8,128)(2,1)}, u32[]{:S(2)}) copy-start(bf16[512,1408]{1,0:T(8,128)(2,1)} %param.13) | copy-start | bytes 4325380
  191.2 93.1 %copy-start.11 = (f32[1408]{0:T(1024)S(1)}, f32[1408]{0:T(1024)}, u32[]{:S(2)}) copy-start(f32[1408]{0:T(1024)} %param.21) | copy-start | bytes 16900
  191.3 180.8 %all-reduce.6.cloned.1.call-start = ((), (), s32[]{:S(2)}) async-start(), calls=%async_computation.2 | async-start | bytes 5767168 | tf_op jit(solution)/shard_map/psum | solution.py:32
  284.3 16.4 %copy-start.12 = (s32[32]{0:T(128)S(1)}, s32[32]{0:T(128)}, u32[]{:S(2)}) copy-start(s32[32]{0:T(128)} %param.15) | copy-start | bytes 388
  300.8 74.7 %copy-start.7 = (f32[1408]{0:T(1024)S(1)}, f32[1408]{0:T(1024)}, u32[]{:S(2)}) copy-start(f32[1408]{0:T(1024)} %param.24) | copy-start | bytes 16900
  389.1 99.7 %all-to-all-start = ((bf16[32,128,896]{2,1,0:T(8,128)(2,1)}), bf16[32,128,896]{2,1,0:T(8,128)(2,1)}, u32[]{:S(2)}, u32[]{:S(2)}) async-start(bf16[32,128,896]{2,1,0:T(8,128)(2,1)} %broadcast_select_fusion), calls=%async_computation | async-start | bytes 14680064 | tf_op jit(solution)/shard_map/all_to_all | solution.py:139
  488.7 2.3 copy-start.1
Sparse Core Ops, SparseCore 0:
  191.4 90.3 all-reduce.3
  300.7 71.2 all-reduce.5
where the time goes:
time: 499 us; the launch traced here: 498 us
  waiting for transfers between devices  272 us (55%)
  matrix products  62.6 us (13%)
  blocking collectives  62.3 us (12%)
  other arithmetic  40.1 us (8%)
  starting transfers between devices  30.1 us (6%)
  between operations  15.8 us (3%)
  local copies, waits for them, and re-layouts  15.2 us (3%)
    psum x2, waiting for transfers between devices, sum_rows(): return lax.psum(partial_value, 'tp')  162 us
    all_to_all x1, waiting for transfers between devices, shards(): lax.all_to_all(outgoing, 'seq', split_axis=0, concat_axis=0, tiled=True)  87.6 us
    all_gather x1, blocking collectives, shards(): group_table = lax.all_gather(group_image, 'seq', axis=0, tiled=True)  62.3 us
    ppermute x8, waiting for transfers between devices, shifted(): lax.ppermute(value, axis, [(source, source + steps) for source in range(i...  22.7 us
    ppermute x8, starting transfers between devices, shifted(): lax.ppermute(value, axis, [(source, source + steps) for source in range(i...  22.5 us
    dot_general x1, matrix products, attend_window(): jnp.einsum('qhd,khd->hqk', query_heads, key_heads, preferred_element_type...  18.3 us
    reduce_sum x1, other arithmetic, attend_window(): row_total = jnp.sum(weights, axis=2)  17.5 us
    dot_general x1, matrix products, shards(): jnp.dot(hidden_units, down_weight, preferred_element_type=jnp.float32)  16.3 us
  transfers between devices with their start and end apart: 11, of which 6 were waited for; matrix products, arithmetic and copies ran while one was open for 3% of the time, Pallas kernels for 0%

commit v1 on v0

--- a/solution.py
+++ b/solution.py
@@ -29,7 +29,7 @@
 
 
 def sum_rows(partial_value):
-    return lax.psum(partial_value, "tp")
+    return jnp.sum(lax.all_gather(partial_value, "tp"), axis=0)
 
 
 def attend_window(query_heads, key_heads, value_heads, query_image, key_image):

time: 499 us -> 591 us (1.18)
  waiting for transfers between devices: 272 us -> 350 us
  other arithmetic: 40.1 us -> 54.1 us
    all_gather x0 -> x2, waiting for transfers between devices: none -> 239 us  [sum_rows(): return jnp.sum(lax.all_gather(partial_value, 'tp'), axis=0)]
    psum x2 -> x0, waiting for transfers between devices: 162 us -> none  [sum_rows(): return lax.psum(partial_value, 'tp')]
    reduce_sum x0 -> x2, other arithmetic: none -> 14 us  [sum_rows(): return jnp.sum(lax.all_gather(partial_value, 'tp'), axis=0)]
where the time goes in v1:
time: 591 us; the launch traced here: 590 us
  waiting for transfers between devices  350 us (59%)
  matrix products  62.6 us (11%)
  blocking collectives  62.3 us (11%)
  other arithmetic  54.1 us (9%)
  starting transfers between devices  30.1 us (5%)
  between operations  15.8 us (3%)
  local copies, waits for them, and re-layouts  15.1 us (3%)
    all_gather x2, waiting for transfers between devices, sum_rows(): return jnp.sum(lax.all_gather(partial_value, 'tp'), axis=0)  239 us
    all_to_all x1, waiting for transfers between devices, shards(): lax.all_to_all(outgoing, 'seq', split_axis=0, concat_axis=0, tiled=True)  87.6 us
    all_gather x1, blocking collectives, shards(): group_table = lax.all_gather(group_image, 'seq', axis=0, tiled=True)  62.3 us
    ppermute x8, waiting for transfers between devices, shifted(): lax.ppermute(value, axis, [(source, source + steps) for source in range(i...  22.7 us
    ppermute x8, starting transfers between devices, shifted(): lax.ppermute(value, axis, [(source, source + steps) for source in range(i...  22.5 us
    dot_general x1, matrix products, attend_window(): jnp.einsum('qhd,khd->hqk', query_heads, key_heads, preferred_element_type...  18.3 us
    reduce_sum x1, other arithmetic, attend_window(): row_total = jnp.sum(weights, axis=2)  17.5 us
    dot_general x1, matrix products, shards(): jnp.dot(hidden_units, down_weight, preferred_element_type=jnp.float32)  16.2 us
  transfers between devices with their start and end apart: 11, of which 6 were waited for; matrix products, arithmetic and copies ran while one was open for 3% of the time, Pallas kernels for 0%

profile of v1, /device:TPU:0, one launch (start us, length us, event | category | flops | bytes accessed | tf_op | source)
XLA Modules:
  0.0 589.6 jit_solution(12941045562943322514)
XLA Ops:
  6.5 2.0 convert_reduce_fusion
  8.6 1.9 fusion.18
  15.2 3.9 collective-permute-start.3
  19.2 3.6 collective-permute-start.2
  22.7 3.9 collective-permute-start.1
  26.6 5.6 collective-permute-start
  32.2 62.3 %all-gather.2 = s32[32,1,128]{2,1,0:T(1,128)S(1)} all-gather(s32[1,1,128]{2,1,0:T(1,128)S(1)} %bitcast.46), channel_id=1, replica_groups=mesh['seq'=32,'tp'=4] {'seq'}, dimensions={0}, use_global_device_ids=true | all-gather | bytes 16896 | tf_op jit(solution)/shard_map/all_gather | solution.py:72
  95.1 1.6 reshape.126
  98.3 3.2 convolution_convert_fusion
  106.5 1.5 collective-permute-start.7
  111.6 11.1 %collective-permute-done.5 = bf16[2,512,352]{1,2,0:T(8,128)(2,1)S(1)} collective-permute-done((bf16[2,512,352]{1,2,0:T(8,128)(2,1)}, bf16[2,512,352]{1,2,0:T(8,128)(2,1)S(1)}, u32[]{:S(2)}, u32[]{:S(2)}) %collective-permute-start.5) | collective-permute-done | bytes 720928 | tf_op jit(solution)/shard_map/ppermute | solution.py:16
  122.7 7.1 %collective-permute-done.6 = bf16[2,512,352]{1,2,0:T(8,128)(2,1)S(1)} collective-permute-done((bf16[2,512,352]{1,2,0:T(8,128)(2,1)}, bf16[2,512,352]{1,2,0:T(8,128)(2,1)S(1)}, u32[]{:S(2)}, u32[]{:S(2)}) %collective-permute-start.6) | collective-permute-done | bytes 720928 | tf_op jit(solution)/shard_map/ppermute | solution.py:16
  129.8 4.5 collective-permute-done.7
  134.4 3.1 fusion.109
  137.6 18.3 %fusion = (f32[4,512]{1,0:T(4,128)S(1)}, f32[4,512,4608]{2,1,0:T(8,128)}) fusion(pred[512,4608]{1,0:T(8,128)(4,1)S(1)} %broadcast_compare_fusion, bf16[512,4,88]{0,2,1:T(8,128)(2,1)S(1)} %bitcast.47, bf16[4608,4,88]{0,2,1:T(8,128)(2,1)} %bitcast.40), kind=kOutput, calls=%fused_computation.2 | convolution fusion | flops 1689253888 | bytes 43720704 | tf_op jit(solution)/shard_map/qhd,khd->hqk/dot_general | solution.py:36
  155.8 17.5 %fusion.1 = f32[4,512]{1,0:T(4,128)S(1)} fusion(f32[4,512,4608]{2,1,0:T(8,128)} %get-tuple-element.23, f32[4,512]{1,0:T(4,128)S(1)} %get-tuple-element.22, pred[512,4608]{1,0:T(8,128)(4,1)S(1)} %broadcast_compare_fusion), kind=kLoop, calls=%fused_computation.3 | loop fusion | flops 37746688 | bytes 40124416 | tf_op jit(solution)/shard_map/reduce_sum | solution.py:43
  173.3 15.3 %fusion.67 = bf16[512,4,88]{0,2,1:T(8,128)(2,1)S(1)} fusion(bf16[4608,4,88]{0,2,1:T(8,128)(2,1)S(1)} %bitcast.39, f32[4,512,4608]{2,1,0:T(8,128)} %get-tuple-element.23, f32[4,512]{1,0:T(4,128)S(1)} %get-tuple-element.22, pred[512,4608]{1,0:T(8,128)(4,1)S(1)} %broadcast_compare_fusion, f32[512,4]{0,1:T(4,128)S(1)} %bitcast.45), kind=kOutput, calls=%fused_computation.84 | convolution fusion | flops 1699053568 | bytes 43728896 | tf_op jit(solution)/shard_map/hqk,khd->qhd/dot_general | solution.py:44
  188.6 2.7 fusion.110
  191.6 128.6 %all-gather.6.cloned.1.call-done = f32[2048,1408]{1,0:T(8,128)} async-done(((f32[512,1408]{1,0:T(8,128)}), f32[2048,1408]{1,0:T(8,128)}) %all-gather.6.cloned.1.call-update) | async-done | bytes 11534352 | tf_op jit(solution)/shard_map/all_gather | solution.py:32
  320.1 7.0 %reduce_sum.123 = f32[512,1408]{1,0:T(8,128)} reduce(f32[4,512,1408]{2,1,0:T(8,128)} %bitcast.38, f32[]{:T(128)} %constant.11.clone.1), dimensions={0}, to_apply=%region_7.8 | reduce | flops 2162688 | bytes 14417924 | tf_op jit(solution)/shard_map/reduce_sum | solution.py:32
  327.1 2.5 fusion.71
  329.6 16.2 %fusion.20 = f32[512,1408]{1,0:T(8,128)} fusion(bf16[1536,1408]{1,0:T(8,128)(2,1)} %param.23, bf16[1408,1536]{1,0:T(8,128)(2,1)} %param.22, f32[1408]{0:T(1024)S(1)} %copy-done.11, f32[512]{0:T(512)S(1)} %get-tuple-element.19, f32[512]{0:T(512)S(1)} %get-tuple-element.18, f32[512,1408]{1,0:T(8,128)} %reduce_sum.123, bf16[512,1408]{1,0:T(8,128)(2,1)S(1)} %copy-done.2), kind=kOutput, calls=%fused_computation.41 | convolution fusion | flops 4484628480 | bytes 15869440 | tf_op jit(solution)/shard_map/dot_general | solution.py:113
  346.0 110.7 %all-gather.8.cloned.1.call-done = f32[2048,1408]{1,0:T(8,128)} async-done(((f32[512,1408]{1,0:T(8,128)}), f32[2048,1408]{1,0:T(8,128)}) %all-gather.8.cloned.1.call-update) | async-done | bytes 11534352 | tf_op jit(solution)/shard_map/all_gather | solution.py:32
  456.7 7.0 %reduce_sum.126 = f32[512,1408]{1,0:T(8,128)} reduce(f32[4,512,1408]{2,1,0:T(8,128)} %bitcast.37, f32[]{:T(128)} %constant.11.clone.1), dimensions={0}, to_apply=%region_10.11 | reduce | flops 2162688 | bytes 14417924 | tf_op jit(solution)/shard_map/reduce_sum | solution.py:32
  463.7 3.4 fusion.107
  467.2 1.6 multiply_convert_fusion
  468.7 2.7 reshape.129
  471.4 5.5 convolution_convert_fusion.3
  477.0 3.8 broadcast_select_fusion
  480.8 7.4 %all-to-all-start = ((bf16[32,128,896]{2,1,0:T(8,128)(2,1)}), bf16[32,128,896]{2,1,0:T(8,128)(2,1)}, u32[]{:S(2)}, u32[]{:S(2)}) async-start(bf16[32,128,896]{2,1,0:T(8,128)(2,1)} %broadcast_select_fusion), calls=%async_computation | async-start | bytes 14680064 | tf_op jit(solution)/shard_map/all_to_all | solution.py:139
  492.9 87.6 %all-to-all-done = bf16[32,128,896]{2,1,0:T(8,128)(2,1)} async-done(((bf16[32,128,896]{2,1,0:T(8,128)(2,1)}), bf16[32,128,896]{2,1,0:T(8,128)(2,1)}, u32[]{:S(2)}, u32[]{:S(2)}) %all-to-all-start) | async-done | bytes 7340064 | tf_op jit(solution)/shard_map/all_to_all | solution.py:139
  580.5 2.3 select_bitcast_fusion
  (66 shorter events, 18.7 us)
Async XLA Ops:
  6.5 182.1 %copy-start = (bf16[352,1408]{1,0:T(8,128)(2,1)S(1)}, bf16[352,1408]{1,0:T(8,128)(2,1)}, u32[]{:S(2)}) copy-start(bf16[352,1408]{1,0:T(8,128)(2,1)} %param.20) | copy-start | bytes 2973700
  6.5 3.9 copy-start.9
  6.5 313.6 %all-gather.6.cloned.1.call-start = ((), (), s32[]{:S(2)}) async-start(), calls=%async_computation.1 | async-start | bytes 14417920 | tf_op jit(solution)/shard_map/all_gather | solution.py:32
  10.5 2.5 copy-start.4
  10.5 1.7 copy-start.10
  12.2 20.1 %copy-start.8 = (s32[128]{0:T(128)S(1)}, s32[128]{0:T(128)}, u32[]{:S(2)}) copy-start(s32[128]{0:T(128)} %param.14) | copy-start | bytes 1540
  13.0 1.0 copy-start.5
  14.0 96.5 %collective-permute-start.4 = (bf16[2,512,352]{1,2,0:T(8,128)(2,1)}, bf16[2,512,352]{1,2,0:T(8,128)(2,1)}, u32[]{:S(2)}, u32[]{:S(2)}) collective-permute-start(bf16[2,512,352]{1,2,0:T(8,128)(2,1)} %pad_maximum_fusion), channel_id=1, source_target_pairs={{4,0},{8,4},{12,8},{16,12},{20,16},{24,20},{28,24},{32,28},{36,32}... | collective-permute-start | bytes 2162696 | tf_op jit(solution)/shard_map/ppermute | solution.py:16
  15.2 93.9 %collective-permute-start.3 = (bf16[2,512,352]{1,2,0:T(8,128)(2,1)}, bf16[2,512,352]{1,2,0:T(8,128)(2,1)}, u32[]{:S(2)}, u32[]{:S(2)}) collective-permute-start(bf16[2,512,352]{1,2,0:T(8,128)(2,1)} %pad_maximum_fusion), channel_id=1, source_target_pairs={{0,4},{4,8},{8,12},{12,16},{16,20},{20,24},{24,28},{28,32},{32,36}... | collective-permute-start | bytes 2162696 | tf_op jit(solution)/shard_map/ppermute | solution.py:16
  19.2 87.4 %collective-permute-start.2 = (bf16[2,512,352]{1,2,0:T(8,128)(2,1)}, bf16[2,512,352]{1,2,0:T(8,128)(2,1)}, u32[]{:S(2)}, u32[]{:S(2)}) collective-permute-start(bf16[2,512,352]{1,2,0:T(8,128)(2,1)} %pad_maximum_fusion), channel_id=1, source_target_pairs={{0,8},{4,12},{8,16},{12,20},{16,24},{20,28},{24,32},{28,36},{32,40... | collective-permute-start | bytes 2162696 | tf_op jit(solution)/shard_map/ppermute | solution.py:16
  22.7 81.3 %collective-permute-start.1 = (bf16[2,512,352]{1,2,0:T(8,128)(2,1)}, bf16[2,512,352]{1,2,0:T(8,128)(2,1)}, u32[]{:S(2)}, u32[]{:S(2)}) collective-permute-start(bf16[2,512,352]{1,2,0:T(8,128)(2,1)} %pad_maximum_fusion), channel_id=1, source_target_pairs={{0,12},{4,16},{8,20},{12,24},{16,28},{20,32},{24,36},{28,40},{32,4... | collective-permute-start | bytes 2162696 | tf_op jit(solution)/shard_map/ppermute | solution.py:16
  26.6 74.9 %collective-permute-start = (bf16[2,512,352]{1,2,0:T(8,128)(2,1)}, bf16[2,512,352]{1,2,0:T(8,128)(2,1)}, u32[]{:S(2)}, u32[]{:S(2)}) collective-permute-start(bf16[2,512,352]{1,2,0:T(8,128)(2,1)} %pad_maximum_fusion), channel_id=1, source_target_pairs={{0,16},{4,20},{8,24},{12,28},{16,32},{20,36},{24,40},{28,44},{32,4... | collective-permute-start | bytes 2162696 | tf_op jit(solution)/shard_map/ppermute | solution.py:16
  101.5 8.9 %copy-start.6 = (bf16[1,512,352]{1,2,0:T(8,128)(2,1)S(1)}, bf16[1,512,352]{1,2,0:T(8,128)(2,1)}, u32[]{:S(2)}) copy-start(bf16[1,512,352]{1,2,0:T(8,128)(2,1)} %copy-done.5) | copy-start | bytes 1081348
  101.5 21.2 %collective-permute-start.5 = (bf16[2,512,352]{1,2,0:T(8,128)(2,1)}, bf16[2,512,352]{1,2,0:T(8,128)(2,1)S(1)}, u32[]{:S(2)}, u32[]{:S(2)}) collective-permute-start(bf16[2,512,352]{1,2,0:T(8,128)(2,1)} %pad_maximum_fusion), channel_id=1, source_target_pairs={{8,0},{12,4},{16,8},{20,12},{24,16},{28,20},{32,24},{36,28},{40,32... | collective-permute-start | bytes 2162696 | tf_op jit(solution)/shard_map/ppermute | solution.py:16
  104.1 25.7 %collective-permute-start.6 = (bf16[2,512,352]{1,2,0:T(8,128)(2,1)}, bf16[2,512,352]{1,2,0:T(8,128)(2,1)S(1)}, u32[]{:S(2)}, u32[]{:S(2)}) collective-permute-start(bf16[2,512,352]{1,2,0:T(8,128)(2,1)} %pad_maximum_fusion), channel_id=1, source_target_pairs={{12,0},{16,4},{20,8},{24,12},{28,16},{32,20},{36,24},{40,28},{44,3... | collective-permute-start | bytes 2162696 | tf_op jit(solution)/shard_map/ppermute | solution.py:16
  106.5 27.8 %collective-permute-start.7 = (bf16[2,512,352]{1,2,0:T(8,128)(2,1)}, bf16[2,512,352]{1,2,0:T(8,128)(2,1)S(1)}, u32[]{:S(2)}, u32[]{:S(2)}) collective-permute-start(bf16[2,512,352]{1,2,0:T(8,128)(2,1)} %pad_maximum_fusion), channel_id=1, source_target_pairs={{16,0},{20,4},{24,8},{28,12},{32,16},{36,20},{40,24},{44,28},{48,3... | collective-permute-start | bytes 2162696 | tf_op jit(solution)/shard_map/ppermute | solution.py:16
  134.4 3.2 copy-start.13
  155.8 17.5 %copy-start.3 = (bf16[1,4608,352]{1,2,0:T(8,128)(2,1)S(1)}, bf16[1,4608,352]{1,2,0:T(8,128)(2,1)}, u32[]{:S(2)}) copy-start(bf16[1,4608,352]{1,2,0:T(8,128)(2,1)} %get-tuple-element.15) | copy-start | bytes 9732100
  191.3 265.4 %all-gather.8.cloned.1.call-start = ((), (), s32[]{:S(2)}) async-start(), calls=%async_computation.2 | async-start | bytes 14417920 | tf_op jit(solution)/shard_map/all_gather | solution.py:32
  320.1 7.0 %copy-start.2 = (bf16[512,1408]{1,0:T(8,128)(2,1)S(1)}, bf16[512,1408]{1,0:T(8,128)(2,1)}, u32[]{:S(2)}) copy-start(bf16[512,1408]{1,0:T(8,128)(2,1)} %param.13) | copy-start | bytes 4325380
  327.1 2.5 copy-start.11
  329.6 16.4 %copy-start.12 = (s32[32]{0:T(128)S(1)}, s32[32]{0:T(128)}, u32[]{:S(2)}) copy-start(s32[32]{0:T(128)} %param.15) | copy-start | bytes 388
  463.7 3.4 copy-start.7
  480.8 99.7 %all-to-all-start = ((bf16[32,128,896]{2,1,0:T(8,128)(2,1)}), bf16[32,128,896]{2,1,0:T(8,128)(2,1)}, u32[]{:S(2)}, u32[]{:S(2)}) async-start(bf16[32,128,896]{2,1,0:T(8,128)(2,1)} %broadcast_select_fusion), calls=%async_computation | async-start | bytes 14680064 | tf_op jit(solution)/shard_map/all_to_all | solution.py:139
  580.5 2.3 copy-start.1
Sparse Core Ops, SparseCore 0:
  191.4 128.6 all-gather.5
  346.0 110.6 all-gather.7
